TPU v7x, 32 devices: a whole 2x2x4 slice. The times are simulated.
32 devices in a mesh: grp: 4 (over y, x), rows: 8 (over z, core).
Axes of the slice: x: 2, y: 2, z: 4, core: 2. Of those that a mesh axis runs over, the one named last changes fastest.
Arguments:
- stationary: bfloat16 [81920, 512], P(('grp', 'rows')), may hold values from -6 to 6
- rotor_rows: bfloat16 [1024, 512], P(('grp', 'rows')), may hold values from -6 to 6
- owners: int32 [1024, 1], P(('grp', 'rows')), may hold values from 0 to 7; in each aligned block of 32 rows (0 to 31, 32 to 63, ...) at most 6 rows name the same one
- counts: int32 [32], P(('grp', 'rows')), may hold values from 24 to 32
- omega: bfloat16 [512, 192], replicated, may hold values from -0.25 to 0.25
Outputs:
- basis_stationary: bfloat16 [81920, 192], P(('grp', 'rows'))
- basis_rotor: bfloat16 [1536, 192], P(('grp', 'rows'))
- factor: float32 [192, 192], replicated
Inputs may be any that keep to these rules, and one draw needn't show every extreme that they name: `owners`: in the rotor rows of one device no owner is named more than 6 times.
All inputs are finite; a program needn't handle non-finite values.
Results may differ from a plain program's by a relative error of at most 0.0056.
Values may be sent and summed in bfloat16 or wider, within the bound.
No kernel may reach another device: no remote copies, remote signals or barrier semaphores. Data moves between devices by JAX's collectives and lax.ppermute only.
A program may use at most 64 MiB of HBM per device.

v0:
```python
import jax
import jax.numpy as jnp
from jax import lax
from jax.sharding import PartitionSpec as P

CAP = 6


def sketch_block(block, omega):
    return jnp.dot(block, omega, preferred_element_type=jnp.float32).astype(jnp.bfloat16)


def per_device(stationary, rotor_rows, owners, counts, omega):
    n_rows = lax.axis_size("rows")
    n_grp = lax.axis_size("grp")
    rot_dev = rotor_rows.shape[0]
    stat_dev = stationary.shape[0]
    total = n_grp * n_rows * (stat_dev + rot_dev)
    targets = owners[:, 0]
    live = lax.iota(jnp.int32, rot_dev) < counts[0]
    onehot = ((targets[:, None] == lax.iota(jnp.int32, n_rows)[None, :]) & live[:, None]).astype(
        jnp.int32
    )
    rank = jnp.sum((jnp.cumsum(onehot, axis=0) - onehot) * onehot, axis=1)
    slot = jnp.where(live, targets * CAP + rank, -1)
    select = (lax.iota(jnp.int32, n_rows * CAP)[:, None] == slot[None, :]).astype(jnp.bfloat16)
    sketch_stat = sketch_block(stationary, omega)
    outgoing = jnp.dot(select, rotor_rows, preferred_element_type=jnp.float32).astype(jnp.bfloat16)
    outgoing = outgoing.reshape(n_rows, CAP, -1)
    arrived_rows = lax.all_to_all(outgoing, "rows", split_axis=0, concat_axis=0, tiled=True)
    arrived = sketch_block(arrived_rows.reshape(n_rows * CAP, -1), omega)
    local = jnp.concatenate([sketch_stat, arrived], axis=0)
    gram = (
        lax.dot_general(local, local, (((0,), (0,)), ((), ())), preferred_element_type=jnp.float32)
        / total
    )
    lower = jnp.linalg.cholesky(lax.psum(gram, ("grp", "rows")))
    solved = lax.linalg.triangular_solve(
        lower, local.astype(jnp.float32).T, left_side=True, lower=True
    )
    basis = solved.T.astype(jnp.bfloat16)
    return (basis[:stat_dev], basis[stat_dev:], lower.T)


def solution(mesh):
    return jax.shard_map(
        per_device,
        mesh=mesh,
        in_specs=(
            P(("grp", "rows"), None),
            P(("grp", "rows"), None),
            P(("grp", "rows"), None),
            P(("grp", "rows")),
            P(),
        ),
        out_specs=(P(("grp", "rows"), None), P(("grp", "rows"), None), P()),
        check_vma=False,
    )
```

profile of v0, /device:TPU:8, one launch (start us, length us, event | category | flops | bytes accessed | tf_op | source)
XLA Modules:
  0.0 226.8 jit_solution(445382293434304383)
XLA Ops:
  8.0 0.7 fusion.12
  8.8 0.8 select_reduce_fusion.2
  9.6 0.7 add_select_fusion
  10.3 0.9 convolution_convert_fusion.2
  11.2 0.7 reshape.49
  11.8 5.3 %all-to-all-start = ((bf16[8,6,512]{2,1,0:T(8,128)(2,1)}), bf16[8,6,512]{2,1,0:T(8,128)(2,1)S(1)}, u32[]{:S(2)}, u32[]{:S(2)}) async-start(bf16[8,6,512]{2,1,0:T(8,128)(2,1)} %reshape.49), calls=%async_computation | async-start | bytes 131072 | tf_op jit(solution)/shard_map/all_to_all | solution.py:30
  17.2 2.9 %convolution_convert_fusion = bf16[2560,192]{0,1:T(8,128)(2,1)} fusion(bf16[2560,512]{1,0:T(8,128)(2,1)S(1)} %copy-done, bf16[512,192]{0,1:T(8,128)(2,1)} %param.9), kind=kOutput, calls=%fused_computation | convolution fusion | flops 503808000 | bytes 3801088 | tf_op jit(solution)/shard_map/dot_general | solution.py:10
  20.1 1.6 all-to-all-done
  21.8 0.2 convolution_convert_fusion.3
  22.1 2.7 %convolution_multiply_fusion = f32[192,192]{0,1:T(8,128)} fusion(bf16[48,192]{0,1:T(8,128)(2,1)S(1)} %copy.20, bf16[2560,192]{0,1:T(8,128)(2,1)} %convolution_convert_fusion), kind=kOutput, calls=%fused_computation.4 | convolution fusion | flops 194322432 | bytes 1148928 | tf_op jit(solution)/shard_map/dot_general | solution.py:34
  24.8 2.3 fusion.2
  27.1 124.5 %all-reduce.5.cloned.1.call-done = f32[192,192]{0,1:T(8,128)} async-done(((f32[192,192]{0,1:T(8,128)}), f32[192,192]{0,1:T(8,128)}) %all-reduce.5.cloned.1.call-update) | async-done | bytes 147472 | tf_op jit(solution)/shard_map/psum | solution.py:37
  151.6 1.0 copy.22
  152.6 1.0 fusion.3
  153.6 11.7 %cholesky.51 = f32[128,128]{1,0:T(8,128)S(1)} custom-call(f32[128,128]{1,0:T(8,128)S(1)} %cholesky.124), custom_call_target="Cholesky" | custom-call | tf_op jit(solution)/shard_map/jit(cholesky)/cholesky | solution.py:37
  165.3 0.6 compare_reduce_fusion.1
  166.0 9.8 %custom-call.14 = f32[1,128,128]{1,2,0:T(8,128)S(1)} custom-call(f32[1,128,128]{2,1,0:T(8,128)S(1)} %get-tuple-element.35), custom_call_target="InvertDiagBlocksLowerTriangular" | custom-call | tf_op jit(solution)/shard_map/jit(cholesky)/cholesky | solution.py:37
  175.8 0.2 constant_dynamic-update-slice_fusion.1
  176.0 0.2 convolution_subtract_fusion.1
  176.2 5.8 %cholesky.110 = f32[64,64]{1,0:T(8,128)S(1)} custom-call(f32[64,64]{1,0:T(8,128)S(1)} %convolution_subtract_fusion.1), custom_call_target="Cholesky" | custom-call | tf_op jit(solution)/shard_map/jit(cholesky)/cholesky | solution.py:37
  182.1 0.6 compare_reduce_fusion
  184.2 0.5 copy-done.2
  184.7 20.3 %custom-call.15 = f32[2,128,128]{1,2,0:T(8,128)} custom-call(f32[2,128,128]{2,1,0:T(8,128)S(1)} %pad_maximum_fusion.2), custom_call_target="InvertDiagBlocksLowerTriangular" | custom-call | tf_op jit(solution)/shard_map/triangular_solve | solution.py:38
  205.0 2.0 fusion.15
  207.0 2.4 %convolution_subtract_fusion = f32[64,2608]{1,0:T(8,128)S(1)} fusion(f32[128,2608]{0,1:T(8,128)S(1)} %get-tuple-element.41, bf16[192,2608]{1,0:T(8,128)(2,1)} %fusion.2, f32[192,192]{1,0:T(8,128)} %copy-done.2), kind=kOutput, calls=%fused_computation.1 | convolution fusion | flops 256710656 | bytes 2379776 | tf_op jit(solution)/shard_map/triangular_solve | solution.py:38
  209.4 2.2 convolution_convert_fusion.1
  211.7 2.1 copy.23
  213.8 1.3 maximum_bitcast_fusion
  215.1 0.6 slice.72
  215.7 1.1 slice.71
  216.9 0.8 copy.25
  217.7 2.3 %copy.24 = bf16[2560,192]{0,1:T(8,128)(2,1)} copy(bf16[2560,192]{1,0:T(8,128)(2,1)} %slice.71) | data formatting | bytes 1966080
  (21 shorter events, 0.5 us)
Async XLA Ops:
  7.2 10.0 %copy-start = (bf16[2560,512]{1,0:T(8,128)(2,1)S(1)}, bf16[2560,512]{1,0:T(8,128)(2,1)}, u32[]{:S(2)}) copy-start(bf16[2560,512]{1,0:T(8,128)(2,1)} %param.5) | copy-start | bytes 7864324
  11.8 10.0 %all-to-all-start = ((bf16[8,6,512]{2,1,0:T(8,128)(2,1)}), bf16[8,6,512]{2,1,0:T(8,128)(2,1)S(1)}, u32[]{:S(2)}, u32[]{:S(2)}) async-start(bf16[8,6,512]{2,1,0:T(8,128)(2,1)} %reshape.49), calls=%async_computation | async-start | bytes 131072 | tf_op jit(solution)/shard_map/all_to_all | solution.py:30
  17.1 134.4 %all-reduce.5.cloned.1.call-start = ((), (), s32[]{:S(2)}) async-start(), calls=%async_computation.1 | async-start | bytes 393216 | tf_op jit(solution)/shard_map/psum | solution.py:37
  17.2 4.6 %copy-start.1 = (bf16[512,192]{0,1:T(8,128)(2,1)S(1)}, bf16[512,192]{0,1:T(8,128)(2,1)}, u32[]{:S(2)}) copy-start(bf16[512,192]{0,1:T(8,128)(2,1)} %param.9) | copy-start | bytes 589828
  184.1 0.7 copy-start.2
Sparse Core Ops, SparseCore 0:
  24.9 126.6 all-reduce.4
where the time goes:
time: 228 us; the launch traced here: 227 us
  waiting for transfers between devices  126 us (55%)
  other arithmetic  56 us (25%)
  between operations  16.3 us (7%)
  matrix products  13.7 us (6%)
  local copies, waits for them, and re-layouts  9.36 us (4%)
  starting transfers between devices  5.33 us (2%)
    psum x1, waiting for transfers between devices, per_device(): lower = jnp.linalg.cholesky(lax.psum(gram, ('grp', 'rows')))  125 us
    another operation x7, other arithmetic, per_device(): lower = jnp.linalg.cholesky(lax.psum(gram, ('grp', 'rows')))  28.7 us
    another operation x5, other arithmetic, per_device(): lax.linalg.triangular_solve(lower, local.astype(jnp.float32).T, left_side...  20.4 us
    another operation x3, matrix products, per_device(): lax.linalg.triangular_solve(lower, local.astype(jnp.float32).T, left_side...  6.65 us
    all_to_all x1, starting transfers between devices, per_device(): lax.all_to_all(outgoing, 'rows', split_axis=0, concat_axis=0, tiled=True)  5.32 us
  transfers between devices with their start and end apart: 2, of which 2 were waited for; matrix products, arithmetic and copies ran while one was open for 2% of the time, Pallas kernels for 0%

commit v1 on v0

--- a/solution.py
+++ b/solution.py
@@ -34,7 +34,7 @@
         lax.dot_general(local, local, (((0,), (0,)), ((), ())), preferred_element_type=jnp.float32)
         / total
     )
-    lower = jnp.linalg.cholesky(lax.psum(gram, ("grp", "rows")))
+    lower = jnp.linalg.cholesky(jnp.sum(lax.all_gather(gram, ("grp", "rows")), axis=0))
     solved = lax.linalg.triangular_solve(
         lower, local.astype(jnp.float32).T, left_side=True, lower=True
     )

time: 228 us -> 172 us (0.75)
  waiting for transfers between devices: 126 us -> 68.2 us
  other arithmetic: 56 us -> 58.3 us
    psum x1 -> x0, waiting for transfers between devices: 125 us -> none  [per_device(): lower = jnp.linalg.cholesky(lax.psum(gram, ('grp', 'rows')))]
    all_gather x0 -> x1, waiting for transfers between devices: none -> 66.5 us  [per_device(): lax.all_gather(gram, ('grp', 'rows'))]
    reduce_sum x0 -> x1, other arithmetic: none -> 3.24 us  [per_device(): jnp.sum(lax.all_gather(gram, ('grp', 'rows')), axis=0)]
  transfers between devices with their start and end apart: 2 -> 2, of which waited for: 2 -> 2; matrix products, arithmetic and copies ran while one was open for 2% -> 3% of each run, Pallas kernels for 0% -> 0%
where the time goes in v1:
time: 172 us; the launch traced here: 170 us
  waiting for transfers between devices  68.2 us (40%)
  other arithmetic  58.3 us (34%)
  between operations  16.3 us (9%)
  matrix products  13.7 us (8%)
  local copies, waits for them, and re-layouts  8.43 us (5%)
  starting transfers between devices  5.33 us (3%)
    all_gather x1, waiting for transfers between devices, per_device(): lax.all_gather(gram, ('grp', 'rows'))  66.5 us
    another operation x7, other arithmetic, per_device(): jnp.linalg.cholesky(jnp.sum(lax.all_gather(gram, ('grp', 'rows')), axis=0))  28.7 us
    another operation x5, other arithmetic, per_device(): lax.linalg.triangular_solve(lower, local.astype(jnp.float32).T, left_side...  20.4 us
    another operation x3, matrix products, per_device(): lax.linalg.triangular_solve(lower, local.astype(jnp.float32).T, left_side...  6.64 us
    all_to_all x1, starting transfers between devices, per_device(): lax.all_to_all(outgoing, 'rows', split_axis=0, concat_axis=0, tiled=True)  5.32 us
    unnamed x8, local copies, waits for them, and re-layouts  3.68 us
  transfers between devices with their start and end apart: 2, of which 2 were waited for; matrix products, arithmetic and copies ran while one was open for 3% of the time, Pallas kernels for 0%

profile of v1, /device:TPU:8, one launch (start us, length us, event | category | flops | bytes accessed | tf_op | source)
XLA Modules:
  0.0 170.2 jit_solution(338510116373406820)
XLA Ops:
  8.0 0.7 fusion.12
  8.8 0.8 select_reduce_fusion.2
  9.6 0.7 add_select_fusion
  10.3 0.9 convolution_convert_fusion.2
  11.2 0.7 reshape.49
  11.8 5.3 %all-to-all-start = ((bf16[8,6,512]{2,1,0:T(8,128)(2,1)}), bf16[8,6,512]{2,1,0:T(8,128)(2,1)S(1)}, u32[]{:S(2)}, u32[]{:S(2)}) async-start(bf16[8,6,512]{2,1,0:T(8,128)(2,1)} %reshape.49), calls=%async_computation | async-start | bytes 131072 | tf_op jit(solution)/shard_map/all_to_all | solution.py:30
  17.2 2.9 %convolution_convert_fusion = bf16[2560,192]{0,1:T(8,128)(2,1)} fusion(bf16[2560,512]{1,0:T(8,128)(2,1)S(1)} %copy-done, bf16[512,192]{0,1:T(8,128)(2,1)} %param.9), kind=kOutput, calls=%fused_computation | convolution fusion | flops 503808000 | bytes 3801088 | tf_op jit(solution)/shard_map/dot_general | solution.py:10
  20.1 1.7 all-to-all-done
  21.8 0.2 convolution_convert_fusion.3
  22.0 0.1 copy.23
  22.1 2.7 %convolution_multiply_fusion = f32[192,192]{1,0:T(8,128)} fusion(bf16[48,192]{0,1:T(8,128)(2,1)S(1)} %copy.23, bf16[2560,192]{0,1:T(8,128)(2,1)} %convolution_convert_fusion), kind=kOutput, calls=%fused_computation.4 | convolution fusion | flops 194322432 | bytes 1148928 | tf_op jit(solution)/shard_map/dot_general | solution.py:34
  24.8 2.3 %fusion.2 = bf16[192,2608]{1,0:T(8,128)(2,1)} fusion(bf16[48,192]{0,1:T(8,128)(2,1)S(1)} %copy.23, bf16[2560,192]{0,1:T(8,128)(2,1)} %convolution_convert_fusion), kind=kLoop, calls=%fused_computation.11 | loop fusion | flops 2002944 | bytes 2002944 | tf_op jit(solution)/shard_map/transpose | solution.py:39
  27.1 66.5 %all-gather.3.cloned.1.call-done = f32[6144,192]{1,0:T(8,128)} async-done(((f32[192,192]{1,0:T(8,128)}), f32[6144,192]{1,0:T(8,128)}) %all-gather.3.cloned.1.call-update) | async-done | bytes 4718608 | tf_op jit(solution)/shard_map/all_gather | solution.py:37
  93.6 3.2 %reduce_sum.19 = f32[192,192]{1,0:T(8,128)S(1)} reduce(f32[32,192,192]{2,1,0:T(8,128)} %bitcast.44, f32[]{:T(128)} %constant.91.clone.1), dimensions={0}, to_apply=%region_2.3 | reduce | flops 1142784 | bytes 4866052 | tf_op jit(solution)/shard_map/reduce_sum | solution.py:37
  97.0 11.7 %cholesky.51 = f32[128,128]{1,0:T(8,128)S(1)} custom-call(f32[128,128]{1,0:T(8,128)S(1)} %cholesky.124), custom_call_target="Cholesky" | custom-call | tf_op jit(solution)/shard_map/jit(cholesky)/cholesky | solution.py:37
  108.7 9.8 %custom-call.14 = f32[1,128,128]{1,2,0:T(8,128)S(1)} custom-call(f32[1,128,128]{2,1,0:T(8,128)S(1)} %get-tuple-element.38), custom_call_target="InvertDiagBlocksLowerTriangular" | custom-call | tf_op jit(solution)/shard_map/jit(cholesky)/cholesky | solution.py:37
  118.5 0.2 constant_dynamic-update-slice_fusion.1
  118.7 0.2 convolution_subtract_fusion.1
  118.9 5.8 %cholesky.110 = f32[64,64]{1,0:T(8,128)S(1)} custom-call(f32[64,64]{1,0:T(8,128)S(1)} %convolution_subtract_fusion.1), custom_call_target="Cholesky" | custom-call | tf_op jit(solution)/shard_map/jit(cholesky)/cholesky | solution.py:37
  124.8 0.6 compare_reduce_fusion
  125.5 0.6 compare_reduce_fusion.1
  127.6 0.5 copy-done.2
  128.1 20.3 %custom-call.15 = f32[2,128,128]{1,2,0:T(8,128)} custom-call(f32[2,128,128]{2,1,0:T(8,128)S(1)} %pad_maximum_fusion.2), custom_call_target="InvertDiagBlocksLowerTriangular" | custom-call | tf_op jit(solution)/shard_map/triangular_solve | solution.py:38
  148.4 2.0 %fusion.15 = (bf16[128,2608]{0,1:T(8,128)(2,1)S(1)}, f32[128,2608]{0,1:T(8,128)S(1)}) fusion(bf16[192,2608]{1,0:T(8,128)(2,1)} %fusion.2, f32[2,128,128]{1,2,0:T(8,128)} %custom-call.15), kind=kOutput, calls=%fused_computation.50 | convolution fusion | flops 513087488 | bytes 2756608 | tf_op jit(solution)/shard_map/triangular_solve | solution.py:38
  150.4 2.4 %convolution_subtract_fusion = f32[64,2608]{1,0:T(8,128)S(1)} fusion(f32[128,2608]{0,1:T(8,128)S(1)} %get-tuple-element.44, bf16[192,2608]{1,0:T(8,128)(2,1)} %fusion.2, f32[192,192]{1,0:T(8,128)} %copy-done.2), kind=kOutput, calls=%fused_computation.1 | convolution fusion | flops 256710656 | bytes 2379776 | tf_op jit(solution)/shard_map/triangular_solve | solution.py:38
  152.8 2.2 %convolution_convert_fusion.1 = bf16[64,2608]{1,0:T(8,128)(2,1)} fusion(f32[64,2608]{1,0:T(8,128)S(1)} %convolution_subtract_fusion, f32[2,128,128]{1,2,0:T(8,128)} %custom-call.15), kind=kOutput, calls=%fused_computation.2 | convolution fusion | flops 128355328 | bytes 1034240 | tf_op jit(solution)/shard_map/triangular_solve | solution.py:38
  155.0 2.1 %copy.25 = bf16[64,2608]{0,1:T(8,128)(2,1)} copy(bf16[64,2608]{1,0:T(8,128)(2,1)} %convolution_convert_fusion.1) | data formatting | bytes 667648 | tf_op jit(solution)/shard_map/convert.7
  157.1 1.3 maximum_bitcast_fusion
  158.5 1.1 slice.71
  159.6 0.6 slice.72
  160.2 2.3 %copy.26 = bf16[2560,192]{0,1:T(8,128)(2,1)} copy(bf16[2560,192]{1,0:T(8,128)(2,1)} %slice.71) | data formatting | bytes 1966080
  162.5 0.8 copy.27
  (22 shorter events, 0.5 us)
Async XLA Ops:
  7.2 10.0 %copy-start = (bf16[2560,512]{1,0:T(8,128)(2,1)S(1)}, bf16[2560,512]{1,0:T(8,128)(2,1)}, u32[]{:S(2)}) copy-start(bf16[2560,512]{1,0:T(8,128)(2,1)} %param.5) | copy-start | bytes 7864324
  11.8 10.0 %all-to-all-start = ((bf16[8,6,512]{2,1,0:T(8,128)(2,1)}), bf16[8,6,512]{2,1,0:T(8,128)(2,1)S(1)}, u32[]{:S(2)}, u32[]{:S(2)}) async-start(bf16[8,6,512]{2,1,0:T(8,128)(2,1)} %reshape.49), calls=%async_computation | async-start | bytes 131072 | tf_op jit(solution)/shard_map/all_to_all | solution.py:30
  17.1 4.7 %copy-start.1 = (bf16[512,192]{0,1:T(8,128)(2,1)S(1)}, bf16[512,192]{0,1:T(8,128)(2,1)}, u32[]{:S(2)}) copy-start(bf16[512,192]{0,1:T(8,128)(2,1)} %param.9) | copy-start | bytes 589828
  17.1 76.4 %all-gather.3.cloned.1.call-start = ((), (), s32[]{:S(2)}) async-start(), calls=%async_computation.1 | async-start | bytes 6488064 | tf_op jit(solution)/shard_map/all_gather | solution.py:37
  127.4 0.7 copy-start.2
Sparse Core Ops, SparseCore 0:
  24.9 68.5 all-gather.2
